TPU v7x, 128 devices: a whole 4x4x4 slice. The times are simulated.
128 devices in a mesh: seq: 128 (over y, x, z, core).
Axes of the slice: x: 4, y: 4, z: 4, core: 2. Of those that a mesh axis runs over, the one named last changes fastest.
Arguments:
- queries: bfloat16 [16384, 8192], P('seq'), may hold values from -5.1 to 5.1
- keys: bfloat16 [16384, 1024], P('seq'), may hold values from -5.1 to 5.1
- values: bfloat16 [16384, 1024], P('seq'), may hold values from -6 to 6
- lengths: int32 [32], replicated, may hold values from 1 to 8, 128 in all
- class_weight: bfloat16 [8192, 16], replicated, may hold values from -0.25 to 0.25
Outputs:
- attended: bfloat16 [16384, 8192], P('seq')
- doc_logits: float32 [128, 16], P('seq')
Inputs may be any that keep to these rules, and one draw needn't show every extreme that they name: `lengths`: lengths are counted in blocks of 128 tokens; they sum to 128 and the longest is exactly 8 blocks.
All inputs are finite; a program needn't handle non-finite values.
Results may differ from a plain program's by a relative error of at most 0.0046.
Values may be sent and summed in bfloat16 or wider, within the bound.
No kernel may reach another device: no remote copies, remote signals or barrier semaphores. Data moves between devices by JAX's collectives and lax.ppermute only.
A program may use at most 192 MiB of HBM per device.

v0:
```python
import jax
import jax.numpy as jnp
from jax import lax
from jax.sharding import PartitionSpec as P
from jax.experimental import pallas as pl
from jax.experimental.pallas import tpu as pltpu

DH = 128
BLK = 128
MAXB = 8


def shifted(block, axis, distance):
    count = lax.axis_size(axis)
    if distance > 0:
        route = [(i - distance, i) for i in range(distance, count)]
    else:
        route = [(i - distance, i) for i in range(0, count + distance)]
    return lax.ppermute(block, axis, route)


def block_docs(lengths, block_count):
    doc_ends = jnp.cumsum(lengths, dtype=jnp.int32)
    doc_firsts = doc_ends - lengths
    blocks = jnp.arange(block_count, dtype=jnp.int32)
    owner_doc = jnp.sum((doc_ends[None, :] <= blocks[:, None]).astype(jnp.int32), axis=1)
    matches = owner_doc[:, None] == jnp.arange(lengths.shape[0], dtype=jnp.int32)[None, :]
    first_block = jnp.sum(jnp.where(matches, doc_firsts[None, :], 0), axis=1)
    return (owner_doc, first_block)


def attention_kernel(meta_ref, q_ref, stack_ref, *refs):
    own = len(refs) - 8
    out_ref, out0_ref, m_ref, l_ref, acc_ref, m0_ref, l0_ref, acc0_ref = refs[own:]
    rows = q_ref.shape[2] // 2
    loaders = [lambda cols, r=r: r[:, cols] for r in refs[:own]]
    loaders += [lambda cols, i=i: stack_ref[i, :, cols] for i in range(stack_ref.shape[0])]
    tiles = len(loaders)
    heads = 2 * q_ref.shape[0]
    width_k = (stack_ref.shape[2] - DH) // 2
    heads_kv = width_k // DH
    group = heads // heads_kv
    factor = DH ** (-0.5)
    q0s_ref = out0_ref

    for t in range(tiles):

        @pl.when(meta_ref[tiles] == t)
        def _(load=loaders[t]):
            q0s_ref[...] = load(pl.ds(2 * width_k, DH)).astype(jnp.float32)

    q0t = q0s_ref[...].astype(jnp.bfloat16)
    column_head = lax.broadcasted_iota(jnp.int32, (1, DH), 1) // group

    def scored(k, vt, qt):
        st = jnp.dot(k, qt, preferred_element_type=jnp.float32) * factor
        m1 = jnp.max(st, axis=0, keepdims=True)
        p = jnp.exp(st - m1)
        l1 = jnp.sum(p, axis=0, keepdims=True)
        ot = jnp.dot(vt, p.astype(jnp.bfloat16), preferred_element_type=jnp.float32)
        return m1, l1, ot

    def merge(first, ms, ls, accs, j, m1, l1, o1, mask=None):
        def put(ref, value):
            if mask is None:
                ref[j] = value
            else:
                ref[j] = jnp.where(mask, value, ref[j])

        if first:
            put(ms, m1)
            put(ls, l1)
            put(accs, o1)
        else:
            m0 = ms[j]
            mn = jnp.maximum(m0, m1)
            a = jnp.exp(m0 - mn)
            b = jnp.exp(m1 - mn)
            put(ms, mn)
            put(ls, ls[j] * a + l1 * b)
            put(accs, accs[j] * a + o1 * b)

    def tile_step(load, first):
        def one_head(h, carry):
            kcol = pl.multiple_of(h * DH, DH)
            vcol = pl.multiple_of(width_k + h * DH, DH)
            k = load(pl.ds(kcol, DH))
            vt = load(pl.ds(vcol, DH)).astype(jnp.float32).T.astype(jnp.bfloat16)
            for g in range(group // 2):
                j = h * (group // 2) + g
                merge(first, m_ref, l_ref, acc_ref, j, *scored(k, vt, q_ref[j]))
            merge(first, m0_ref, l0_ref, acc0_ref, 0, *scored(k, vt, q0t), mask=column_head == h)
            return carry

        lax.fori_loop(0, heads_kv, one_head, 0)

    tile_step(loaders[0], True)
    for t in range(1, tiles):

        @pl.when(meta_ref[t] > 0)
        def _(load=loaders[t]):
            tile_step(load, False)

    def finish(j, carry):
        normed = (acc_ref[j] / l_ref[j]).T.astype(out_ref.dtype)
        out_ref[:, pl.ds(pl.multiple_of(2 * j * DH, DH), DH)] = normed[:rows]
        out_ref[:, pl.ds(pl.multiple_of((2 * j + 1) * DH, DH), DH)] = normed[rows:]
        return carry

    lax.fori_loop(0, heads // 2, finish, 0)
    out0_ref[...] = acc0_ref[0] / l0_ref[0]


def attend(meta, q_heads, partner_stack, pieces):
    heads, _, rows = q_heads.shape
    heads, rows = 2 * heads, rows // 2
    return pl.pallas_call(
        attention_kernel,
        out_shape=(
            jax.ShapeDtypeStruct((rows, heads * DH), jnp.bfloat16),
            jax.ShapeDtypeStruct((DH, DH), jnp.float32),
        ),
        in_specs=[pl.BlockSpec(memory_space=pltpu.SMEM)]
        + [pl.BlockSpec(memory_space=pltpu.VMEM)] * (2 + len(pieces)),
        out_specs=(pl.BlockSpec(memory_space=pltpu.VMEM), pl.BlockSpec(memory_space=pltpu.VMEM)),
        scratch_shapes=[
            pltpu.VMEM((heads // 2, 1, 2 * rows), jnp.float32),
            pltpu.VMEM((heads // 2, 1, 2 * rows), jnp.float32),
            pltpu.VMEM((heads // 2, DH, 2 * rows), jnp.float32),
            pltpu.VMEM((1, 1, DH), jnp.float32),
            pltpu.VMEM((1, 1, DH), jnp.float32),
            pltpu.VMEM((1, DH, DH), jnp.float32),
        ],
        compiler_params=pltpu.CompilerParams(vmem_limit_bytes=56 * 1024 * 1024),
    )(meta, q_heads, partner_stack, *pieces)


def shards(queries, keys, values, lengths, class_weight):
    devices = lax.axis_size("seq")
    myself = lax.axis_index("seq")
    row_count = queries.shape[0]
    width_q = queries.shape[1]
    width_k = keys.shape[1]
    heads = width_q // DH
    heads_kv = width_k // DH
    group = heads // heads_kv
    arrived = lax.all_to_all(
        jnp.concatenate(
            [
                queries.reshape(devices, heads, DH),
                keys.reshape(devices, heads_kv, DH),
                values.reshape(devices, heads_kv, DH),
            ],
            axis=1,
        ),
        "seq",
        split_axis=0,
        concat_axis=0,
        tiled=True,
    )
    owner_doc, first_block = block_docs(lengths, devices)
    my_doc = owner_doc[myself]
    partner = myself + 1 - 2 * (myself % 2)
    hops = MAXB // 2
    offsets = [0]
    for hop in range(1, hops):
        offsets += [-2 * hop, 2 * hop]
    offsets = jnp.array(offsets + [0], jnp.int32)
    last = jnp.array([0] * (2 * hops - 1) + [2 * hops], jnp.int32)
    blocks = jnp.concatenate(
        [myself + offsets + last * (1 - 2 * (myself % 2)), partner + offsets + last * (1 - 2 * (partner % 2))]
    )
    inside = (blocks >= 0) & (blocks < devices)
    docs = jnp.take(owner_doc, jnp.clip(blocks, 0, devices - 1))
    flags = (inside & (docs == my_doc)).astype(jnp.int32).at[0].set(1)
    pick = jnp.argmax(blocks == first_block[myself]).astype(jnp.int32)
    meta = jnp.concatenate([flags, pick[None]])
    q_heads = (
        arrived[:, :heads]
        .reshape(row_count, heads // 2, 2, DH)
        .transpose(1, 3, 2, 0)
        .reshape(heads // 2, DH, 2 * row_count)
    )
    own_q0t = jnp.pad(arrived[0, :heads].T, ((0, 0), (0, DH - heads)))
    kv = jnp.concatenate([arrived[:, heads:].reshape(row_count, 2 * width_k), own_q0t], axis=1)
    kv, meta = lax.optimization_barrier((kv, meta))
    pieces = [kv]
    right = kv
    left = kv
    for hop in range(1, hops):
        right = shifted(right, "seq", 2)
        left = shifted(left, "seq", -2)
        pieces += [right, left]
    onward = jnp.where(myself % 2 == 1, right, left)
    route = [(i, i + 2) for i in range(1, devices - 2, 2)] + [(i, i - 2) for i in range(2, devices, 2)]
    pieces.append(lax.ppermute(onward, "seq", route))
    partner_stack = lax.ppermute(
        jnp.stack(pieces), "seq", [(i, i + 1 - 2 * (i % 2)) for i in range(devices)]
    )
    attended, start_out = attend(meta, q_heads, partner_stack, pieces)
    start_row = start_out[:, :heads].T.reshape(1, width_q).astype(jnp.bfloat16)
    doc_logits = jnp.dot(start_row, class_weight, preferred_element_type=jnp.float32)
    return (attended, doc_logits)


def solution(mesh):
    return jax.shard_map(
        shards,
        mesh=mesh,
        in_specs=(P("seq", None), P("seq", None), P("seq", None), P(), P()),
        out_specs=(P("seq", None), P("seq", None)),
        check_vma=False,
    )
```

profile of v0, /device:TPU:25, one launch (start us, length us, event | category | flops | bytes accessed | tf_op | source)
XLA Modules:
  0.0 186.5 jit_solution(12201395597594994156)
XLA Ops:
  2.9 4.1 %copy.34 = bf16[128,8192]{0,1:T(8,128)(2,1)} copy(bf16[128,8192]{1,0:T(8,128)(2,1)} %param.9) | data formatting | bytes 4194304 | tf_op args[0]
  7.0 1.9 %pad_maximum_fusion = bf16[128,80,128]{0,2,1:T(8,128)(2,1)S(1)} fusion(bf16[128,8,128]{0,2,1:T(8,128)(2,1)S(1)} %bitcast.46, bf16[128,8,128]{0,2,1:T(8,128)(2,1)S(1)} %bitcast.45, bf16[128,64,128]{0,2,1:T(8,128)(2,1)} %bitcast.42), kind=kLoop, calls=%fused_computation.1 | loop fusion | flops 2621440 | bytes 5242880 | tf_op jit(solution)/shard_map/concatenate | solution.py:148
  9.0 3.3 %copy.37 = bf16[128,80,128]{2,1,0:T(8,128)(2,1)} copy(bf16[128,80,128]{0,2,1:T(8,128)(2,1)S(1)} %pad_maximum_fusion) | data formatting | bytes 5242880 | tf_op jit(solution)/shard_map/concatenate | solution.py:148
  12.3 10.6 %all-to-all-start = ((bf16[128,80,128]{2,1,0:T(8,128)(2,1)}), bf16[128,80,128]{2,1,0:T(8,128)(2,1)S(1)}, u32[]{:S(2)}, u32[]{:S(2)}) async-start(bf16[128,80,128]{2,1,0:T(8,128)(2,1)} %copy.37), calls=%async_computation | async-start | bytes 5242880 | tf_op jit(solution)/shard_map/all_to_all | solution.py:147
  26.0 1.4 compare_reduce_fusion
  28.5 28.1 %all-to-all-done = bf16[128,80,128]{2,1,0:T(8,128)(2,1)S(1)} async-done(((bf16[128,80,128]{2,1,0:T(8,128)(2,1)}), bf16[128,80,128]{2,1,0:T(8,128)(2,1)S(1)}, u32[]{:S(2)}, u32[]{:S(2)}) %all-to-all-start) | async-done | bytes 2621472 | tf_op jit(solution)/shard_map/all_to_all | solution.py:147
  56.8 1.2 copy.46
  58.0 1.2 copy.40
  59.3 3.4 %collective-permute-start.1 = (bf16[128,2176]{1,0:T(8,128)(2,1)S(1)}, bf16[128,2176]{1,0:T(8,128)(2,1)S(1)}, u32[]{:S(2)}, u32[]{:S(2)}) collective-permute-start(bf16[128,2176]{1,0:T(8,128)(2,1)S(1)} %fusion.1.refs_0_), channel_id=1, source_target_pairs={{2,0},{3,1},{4,2},{5,3},{6,4},{7,5},{8,6},{9,7},{10,8},{11,9},{12,... | collective-permute-start | bytes 1671176 | tf_op jit(solution)/shard_map/ppermute | solution.py:19
  62.8 1.9 %collective-permute-start = (bf16[128,2176]{1,0:T(8,128)(2,1)S(1)}, bf16[128,2176]{1,0:T(8,128)(2,1)S(1)}, u32[]{:S(2)}, u32[]{:S(2)}) collective-permute-start(bf16[128,2176]{1,0:T(8,128)(2,1)S(1)} %fusion.1.refs_0_), channel_id=1, source_target_pairs={{0,2},{1,3},{2,4},{3,5},{4,6},{5,7},{6,8},{7,9},{8,10},{9,11},{10,... | collective-permute-start | bytes 1671176 | tf_op jit(solution)/shard_map/ppermute | solution.py:19
  65.5 8.7 %collective-permute-done.1.refs_2_ = bf16[128,2176]{1,0:T(8,128)(2,1)S(1)} collective-permute-done((bf16[128,2176]{1,0:T(8,128)(2,1)S(1)}, bf16[128,2176]{1,0:T(8,128)(2,1)S(1)}, u32[]{:S(2)}, u32[]{:S(2)}) %collective-permute-start.1) | collective-permute-done | bytes 557088 | tf_op jit(solution)/shard_map/ppermute | solution.py:19
  74.2 8.3 %collective-permute-start.3 = (bf16[128,2176]{1,0:T(8,128)(2,1)S(1)}, bf16[128,2176]{1,0:T(8,128)(2,1)S(1)}, u32[]{:S(2)}, u32[]{:S(2)}) collective-permute-start(bf16[128,2176]{1,0:T(8,128)(2,1)S(1)} %collective-permute-done.1.refs_2_), channel_id=1, source_target_pairs={{2,0},{3,1},{4,2},{5,3},{6,4},{7,5},{8,6},{9,7},{10,8},{11,9},{12,... | collective-permute-start | bytes 1671176 | tf_op jit(solution)/shard_map/ppermute | solution.py:19
  82.5 1.9 %collective-permute-start.2 = (bf16[128,2176]{1,0:T(8,128)(2,1)S(1)}, bf16[128,2176]{1,0:T(8,128)(2,1)S(1)}, u32[]{:S(2)}, u32[]{:S(2)}) collective-permute-start(bf16[128,2176]{1,0:T(8,128)(2,1)S(1)} %collective-permute-done.refs_1_), channel_id=1, source_target_pairs={{0,2},{1,3},{2,4},{3,5},{4,6},{5,7},{6,8},{7,9},{8,10},{9,11},{10,... | collective-permute-start | bytes 1671176 | tf_op jit(solution)/shard_map/ppermute | solution.py:19
  86.2 6.9 %collective-permute-done.3.refs_4_ = bf16[128,2176]{1,0:T(8,128)(2,1)S(1)} collective-permute-done((bf16[128,2176]{1,0:T(8,128)(2,1)S(1)}, bf16[128,2176]{1,0:T(8,128)(2,1)S(1)}, u32[]{:S(2)}, u32[]{:S(2)}) %collective-permute-start.3) | collective-permute-done | bytes 557088 | tf_op jit(solution)/shard_map/ppermute | solution.py:19
  93.1 8.3 %collective-permute-start.5 = (bf16[128,2176]{1,0:T(8,128)(2,1)S(1)}, bf16[128,2176]{1,0:T(8,128)(2,1)S(1)}, u32[]{:S(2)}, u32[]{:S(2)}) collective-permute-start(bf16[128,2176]{1,0:T(8,128)(2,1)S(1)} %collective-permute-done.3.refs_4_), channel_id=1, source_target_pairs={{2,0},{3,1},{4,2},{5,3},{6,4},{7,5},{8,6},{9,7},{10,8},{11,9},{12,... | collective-permute-start | bytes 1671176 | tf_op jit(solution)/shard_map/ppermute | solution.py:19
  101.4 1.9 %collective-permute-start.4 = (bf16[128,2176]{1,0:T(8,128)(2,1)S(1)}, bf16[128,2176]{1,0:T(8,128)(2,1)S(1)}, u32[]{:S(2)}, u32[]{:S(2)}) collective-permute-start(bf16[128,2176]{1,0:T(8,128)(2,1)S(1)} %collective-permute-done.2.refs_3_), channel_id=1, source_target_pairs={{0,2},{1,3},{2,4},{3,5},{4,6},{5,7},{6,8},{7,9},{8,10},{9,11},{10,... | collective-permute-start | bytes 1671176 | tf_op jit(solution)/shard_map/ppermute | solution.py:19
  105.1 6.0 %collective-permute-done.5.refs_6_ = bf16[128,2176]{1,0:T(8,128)(2,1)S(1)} collective-permute-done((bf16[128,2176]{1,0:T(8,128)(2,1)S(1)}, bf16[128,2176]{1,0:T(8,128)(2,1)S(1)}, u32[]{:S(2)}, u32[]{:S(2)}) %collective-permute-start.5) | collective-permute-done | bytes 557088 | tf_op jit(solution)/shard_map/ppermute | solution.py:19
  111.1 8.1 %collective-permute-done.4.refs_5_ = bf16[128,2176]{1,0:T(8,128)(2,1)S(1)} collective-permute-done((bf16[128,2176]{1,0:T(8,128)(2,1)S(1)}, bf16[128,2176]{1,0:T(8,128)(2,1)S(1)}, u32[]{:S(2)}, u32[]{:S(2)}) %collective-permute-start.4) | collective-permute-done | bytes 557088 | tf_op jit(solution)/shard_map/ppermute | solution.py:19
  119.3 1.9 %collective-permute-start.6 = (bf16[128,2176]{1,0:T(8,128)(2,1)S(1)}, bf16[128,2176]{1,0:T(8,128)(2,1)S(1)}, u32[]{:S(2)}, u32[]{:S(2)}) collective-permute-start(bf16[128,2176]{1,0:T(8,128)(2,1)S(1)} %broadcast_select_fusion), channel_id=1, source_target_pairs={{1,3},{3,5},{5,7},{7,9},{9,11},{11,13},{13,15},{15,17},{17,19},{19... | collective-permute-start | bytes 1671176 | tf_op jit(solution)/shard_map/ppermute | solution.py:196
  122.9 10.9 %collective-permute-done.6.refs_7_ = bf16[128,2176]{1,0:T(8,128)(2,1)S(1)} collective-permute-done((bf16[128,2176]{1,0:T(8,128)(2,1)S(1)}, bf16[128,2176]{1,0:T(8,128)(2,1)S(1)}, u32[]{:S(2)}, u32[]{:S(2)}) %collective-permute-start.6) | collective-permute-done | bytes 557088 | tf_op jit(solution)/shard_map/ppermute | solution.py:196
  135.5 1.4 copy.48
  136.8 3.0 %copy.45.q_ref = bf16[32,128,256]{2,1,0:T(8,128)(2,1)} copy(bf16[32,128,256]{1,2,0:T(8,128)(2,1)S(1)} %bitcast.43) | data formatting | bytes 4194304 | tf_op jit(solution)/shard_map/reshape | solution.py:182
  139.9 2.9 %collective-permute-done.7.stack_ref = bf16[8,128,2176]{2,1,0:T(8,128)(2,1)} collective-permute-done((bf16[8,128,2176]{2,1,0:T(8,128)(2,1)}, bf16[8,128,2176]{2,1,0:T(8,128)(2,1)}, u32[]{:S(2)}, u32[]{:S(2)}) %collective-permute-start.7) | collective-permute-done | bytes 4456480 | tf_op jit(solution)/shard_map/ppermute | solution.py:197
  142.7 42.0 %shard_map.86 = (bf16[128,8192]{1,0:T(8,128)(2,1)}, f32[128,128]{1,0:T(8,128)}) custom-call(s32[17]{0:T(128)} %pad_add_fusion.1.meta_ref, bf16[32,128,256]{2,1,0:T(8,128)(2,1)} %copy.45.q_ref, bf16[8,128,2176]{2,1,0:T(8,128)(2,1)} %collective-permute-done.7.stack_ref, bf16[128,2176]{1,0:T(8,128)(2,1)} %copy-done.3, bf16[128,2176]{1,0:T(8,128)(2,1)} %copy-done.5, ...), custom_call_target="tpu_custom_call" | custom-call | tf_op jit(solution)/shard_map/pallas_call | solution.py:117
  (62 shorter events, 16.2 us)
Async XLA Ops:
  0.6 185.1 %copy-start = (bf16[8192,16]{0,1:T(8,128)(2,1)S(1)}, bf16[8192,16]{0,1:T(8,128)(2,1)}, u32[]{:S(2)}) copy-start(bf16[8192,16]{0,1:T(8,128)(2,1)} %param.13) | copy-start | bytes 786436
  8.9 14.0 %copy-start.9 = (s32[32]{0:T(128)S(1)}, s32[32]{0:T(128)}, u32[]{:S(2)}) copy-start(s32[32]{0:T(128)} %param.12) | copy-start | bytes 388
  8.9 14.9 %copy-start.10 = (s32[8]{0:T(128)S(1)}, s32[8]{0:T(128)}, u32[]{:S(2)}) copy-start(s32[8]{0:T(128)} %constant.85.clone) | copy-start | bytes 100
  9.0 14.9 %copy-start.11 = (s32[8]{0:T(128)S(1)}, s32[8]{0:T(128)}, u32[]{:S(2)}) copy-start(s32[8]{0:T(128)} %constant.84.clone) | copy-start | bytes 100
  12.3 44.3 %all-to-all-start = ((bf16[128,80,128]{2,1,0:T(8,128)(2,1)}), bf16[128,80,128]{2,1,0:T(8,128)(2,1)S(1)}, u32[]{:S(2)}, u32[]{:S(2)}) async-start(bf16[128,80,128]{2,1,0:T(8,128)(2,1)} %copy.37), calls=%async_computation | async-start | bytes 5242880 | tf_op jit(solution)/shard_map/all_to_all | solution.py:147
  59.3 42.1 %copy-start.3 = (bf16[128,2176]{1,0:T(8,128)(2,1)}, bf16[128,2176]{1,0:T(8,128)(2,1)S(1)}, u32[]{:S(2)}) copy-start(bf16[128,2176]{1,0:T(8,128)(2,1)S(1)} %fusion.1.refs_0_) | copy-start | bytes 1671172
  59.3 14.9 %collective-permute-start.1 = (bf16[128,2176]{1,0:T(8,128)(2,1)S(1)}, bf16[128,2176]{1,0:T(8,128)(2,1)S(1)}, u32[]{:S(2)}, u32[]{:S(2)}) collective-permute-start(bf16[128,2176]{1,0:T(8,128)(2,1)S(1)} %fusion.1.refs_0_), channel_id=1, source_target_pairs={{2,0},{3,1},{4,2},{5,3},{6,4},{7,5},{8,6},{9,7},{10,8},{11,9},{12,... | collective-permute-start | bytes 1671176 | tf_op jit(solution)/shard_map/ppermute | solution.py:19
  62.8 19.8 %collective-permute-start = (bf16[128,2176]{1,0:T(8,128)(2,1)S(1)}, bf16[128,2176]{1,0:T(8,128)(2,1)S(1)}, u32[]{:S(2)}, u32[]{:S(2)}) collective-permute-start(bf16[128,2176]{1,0:T(8,128)(2,1)S(1)} %fusion.1.refs_0_), channel_id=1, source_target_pairs={{0,2},{1,3},{2,4},{3,5},{4,6},{5,7},{6,8},{7,9},{8,10},{9,11},{10,... | collective-permute-start | bytes 1671176 | tf_op jit(solution)/shard_map/ppermute | solution.py:19
  74.2 60.6 %copy-start.4 = (bf16[128,2176]{1,0:T(8,128)(2,1)}, bf16[128,2176]{1,0:T(8,128)(2,1)S(1)}, u32[]{:S(2)}) copy-start(bf16[128,2176]{1,0:T(8,128)(2,1)S(1)} %collective-permute-done.1.refs_2_) | copy-start | bytes 1671172
  74.2 18.9 %collective-permute-start.3 = (bf16[128,2176]{1,0:T(8,128)(2,1)S(1)}, bf16[128,2176]{1,0:T(8,128)(2,1)S(1)}, u32[]{:S(2)}, u32[]{:S(2)}) collective-permute-start(bf16[128,2176]{1,0:T(8,128)(2,1)S(1)} %collective-permute-done.1.refs_2_), channel_id=1, source_target_pairs={{2,0},{3,1},{4,2},{5,3},{6,4},{7,5},{8,6},{9,7},{10,8},{11,9},{12,... | collective-permute-start | bytes 1671176 | tf_op jit(solution)/shard_map/ppermute | solution.py:19
  82.5 52.2 %copy-start.5 = (bf16[128,2176]{1,0:T(8,128)(2,1)}, bf16[128,2176]{1,0:T(8,128)(2,1)S(1)}, u32[]{:S(2)}) copy-start(bf16[128,2176]{1,0:T(8,128)(2,1)S(1)} %collective-permute-done.refs_1_) | copy-start | bytes 1671172
  82.5 18.9 %collective-permute-start.2 = (bf16[128,2176]{1,0:T(8,128)(2,1)S(1)}, bf16[128,2176]{1,0:T(8,128)(2,1)S(1)}, u32[]{:S(2)}, u32[]{:S(2)}) collective-permute-start(bf16[128,2176]{1,0:T(8,128)(2,1)S(1)} %collective-permute-done.refs_1_), channel_id=1, source_target_pairs={{0,2},{1,3},{2,4},{3,5},{4,6},{5,7},{6,8},{7,9},{8,10},{9,11},{10,... | collective-permute-start | bytes 1671176 | tf_op jit(solution)/shard_map/ppermute | solution.py:19
  93.1 41.7 %copy-start.6 = (bf16[128,2176]{1,0:T(8,128)(2,1)}, bf16[128,2176]{1,0:T(8,128)(2,1)S(1)}, u32[]{:S(2)}) copy-start(bf16[128,2176]{1,0:T(8,128)(2,1)S(1)} %collective-permute-done.3.refs_4_) | copy-start | bytes 1671172
  93.1 18.0 %collective-permute-start.5 = (bf16[128,2176]{1,0:T(8,128)(2,1)S(1)}, bf16[128,2176]{1,0:T(8,128)(2,1)S(1)}, u32[]{:S(2)}, u32[]{:S(2)}) collective-permute-start(bf16[128,2176]{1,0:T(8,128)(2,1)S(1)} %collective-permute-done.3.refs_4_), channel_id=1, source_target_pairs={{2,0},{3,1},{4,2},{5,3},{6,4},{7,5},{8,6},{9,7},{10,8},{11,9},{12,... | collective-permute-start | bytes 1671176 | tf_op jit(solution)/shard_map/ppermute | solution.py:19
  101.4 33.3 %copy-start.7 = (bf16[128,2176]{1,0:T(8,128)(2,1)}, bf16[128,2176]{1,0:T(8,128)(2,1)S(1)}, u32[]{:S(2)}) copy-start(bf16[128,2176]{1,0:T(8,128)(2,1)S(1)} %collective-permute-done.2.refs_3_) | copy-start | bytes 1671172
  101.4 17.8 %collective-permute-start.4 = (bf16[128,2176]{1,0:T(8,128)(2,1)S(1)}, bf16[128,2176]{1,0:T(8,128)(2,1)S(1)}, u32[]{:S(2)}, u32[]{:S(2)}) collective-permute-start(bf16[128,2176]{1,0:T(8,128)(2,1)S(1)} %collective-permute-done.2.refs_3_), channel_id=1, source_target_pairs={{0,2},{1,3},{2,4},{3,5},{4,6},{5,7},{6,8},{7,9},{8,10},{9,11},{10,... | collective-permute-start | bytes 1671176 | tf_op jit(solution)/shard_map/ppermute | solution.py:19
  111.1 24.3 %copy-start.1 = (bf16[128,2176]{1,0:T(8,128)(2,1)}, bf16[128,2176]{1,0:T(8,128)(2,1)S(1)}, u32[]{:S(2)}) copy-start(bf16[128,2176]{1,0:T(8,128)(2,1)S(1)} %collective-permute-done.5.refs_6_) | copy-start | bytes 1671172
  119.2 15.5 %copy-start.2 = (bf16[128,2176]{1,0:T(8,128)(2,1)}, bf16[128,2176]{1,0:T(8,128)(2,1)S(1)}, u32[]{:S(2)}) copy-start(bf16[128,2176]{1,0:T(8,128)(2,1)S(1)} %collective-permute-done.4.refs_5_) | copy-start | bytes 1671172
  119.3 14.5 %collective-permute-start.6 = (bf16[128,2176]{1,0:T(8,128)(2,1)S(1)}, bf16[128,2176]{1,0:T(8,128)(2,1)S(1)}, u32[]{:S(2)}, u32[]{:S(2)}) collective-permute-start(bf16[128,2176]{1,0:T(8,128)(2,1)S(1)} %broadcast_select_fusion), channel_id=1, source_target_pairs={{1,3},{3,5},{5,7},{7,9},{9,11},{11,13},{13,15},{15,17},{17,19},{19... | collective-permute-start | bytes 1671176 | tf_op jit(solution)/shard_map/ppermute | solution.py:196
  133.8 1.1 copy-start.8
  134.9 7.9 %collective-permute-start.7 = (bf16[8,128,2176]{2,1,0:T(8,128)(2,1)}, bf16[8,128,2176]{2,1,0:T(8,128)(2,1)}, u32[]{:S(2)}, u32[]{:S(2)}) collective-permute-start(bf16[8,128,2176]{2,1,0:T(8,128)(2,1)} %bitcast_dynamic-update-slice_fusion), channel_id=1, source_target_pairs={{0,1},{1,0},{2,3},{3,2},{4,5},{5,4},{6,7},{7,6},{8,9},{9,8},{10,11... | collective-permute-start | bytes 13369352 | tf_op jit(solution)/shard_map/ppermute | solution.py:197
where the time goes:
time: 185 us; the launch traced here: 186 us
  waiting for transfers between devices  71.5 us (39%)
  Pallas kernels  42 us (23%)
  starting transfers between devices  38.6 us (21%)
  local copies, waits for them, and re-layouts  26.9 us (15%)
  other arithmetic  5.72 us (3%)
    pallas_call x1, Pallas kernels, attend(): pl.pallas_call(attention_kernel, out_shape=(jax.ShapeDtypeStruct((rows, h...  42 us
    ppermute x6, waiting for transfers between devices, shifted(): return lax.ppermute(block, axis, route)  29.7 us
    all_to_all x1, waiting for transfers between devices, shards(): lax.all_to_all(jnp.concatenate([queries.reshape(devices, heads, DH), keys...  28.1 us
    ppermute x6, starting transfers between devices, shifted(): return lax.ppermute(block, axis, route)  25.8 us
    unnamed x37, local copies, waits for them, and re-layouts  15.2 us
    ppermute x1, waiting for transfers between devices, shards(): pieces.append(lax.ppermute(onward, 'seq', route))  10.9 us
    all_to_all x1, starting transfers between devices, shards(): lax.all_to_all(jnp.concatenate([queries.reshape(devices, heads, DH), keys...  10.6 us
  transfers between devices with their start and end apart: 9, of which 7 were waited for; matrix products, arithmetic and copies ran while one was open for 9% of the time, Pallas kernels for 0%

commit v1 on v0

--- a/solution.py
+++ b/solution.py
@@ -102,7 +102,7 @@
             tile_step(load, False)
 
     def finish(j, carry):
-        normed = (acc_ref[j] / l_ref[j]).T.astype(out_ref.dtype)
+        normed = (acc_ref[j] * (1.0 / l_ref[j])).T.astype(out_ref.dtype)
         out_ref[:, pl.ds(pl.multiple_of(2 * j * DH, DH), DH)] = normed[:rows]
         out_ref[:, pl.ds(pl.multiple_of((2 * j + 1) * DH, DH), DH)] = normed[rows:]
         return carry

time: 185 us -> 186 us (level)
  the two profiles are of different devices: /device:TPU:25 before, /device:TPU:16 now
where the time goes in v1:
time: 186 us; the launch traced here: 185 us
  waiting for transfers between devices  69.5 us (37%)
  Pallas kernels  42.1 us (23%)
  starting transfers between devices  39.1 us (21%)
  local copies, waits for them, and re-layouts  26.9 us (14%)
  other arithmetic  5.72 us (3%)
    pallas_call x1, Pallas kernels, attend(): pl.pallas_call(attention_kernel, out_shape=(jax.ShapeDtypeStruct((rows, h...  42.1 us
    ppermute x6, waiting for transfers between devices, shifted(): return lax.ppermute(block, axis, route)  30 us
    all_to_all x1, waiting for transfers between devices, shards(): lax.all_to_all(jnp.concatenate([queries.reshape(devices, heads, DH), keys...  28.5 us
    ppermute x6, starting transfers between devices, shifted(): return lax.ppermute(block, axis, route)  26.9 us
    unnamed x37, local copies, waits for them, and re-layouts  15.2 us
    all_to_all x1, starting transfers between devices, shards(): lax.all_to_all(jnp.concatenate([queries.reshape(devices, heads, DH), keys...  10.3 us
    ppermute x1, waiting for transfers between devices, shards(): pieces.append(lax.ppermute(onward, 'seq', route))  7.79 us
  transfers between devices with their start and end apart: 9, of which 7 were waited for; matrix products, arithmetic and copies ran while one was open for 9% of the time, Pallas kernels for 0%

profile of v1, /device:TPU:16, one launch (start us, length us, event | category | flops | bytes accessed | tf_op | source)
XLA Modules:
  0.0 185.1 jit_solution(2923700790788090451)
XLA Ops:
  2.9 4.1 %copy.34 = bf16[128,8192]{0,1:T(8,128)(2,1)} copy(bf16[128,8192]{1,0:T(8,128)(2,1)} %param.9) | data formatting | bytes 4194304 | tf_op args[0]
  7.0 1.9 %pad_maximum_fusion = bf16[128,80,128]{0,2,1:T(8,128)(2,1)S(1)} fusion(bf16[128,8,128]{0,2,1:T(8,128)(2,1)S(1)} %bitcast.46, bf16[128,8,128]{0,2,1:T(8,128)(2,1)S(1)} %bitcast.45, bf16[128,64,128]{0,2,1:T(8,128)(2,1)} %bitcast.42), kind=kLoop, calls=%fused_computation.1 | loop fusion | flops 2621440 | bytes 5242880 | tf_op jit(solution)/shard_map/concatenate | solution.py:148
  9.0 3.3 %copy.37 = bf16[128,80,128]{2,1,0:T(8,128)(2,1)} copy(bf16[128,80,128]{0,2,1:T(8,128)(2,1)S(1)} %pad_maximum_fusion) | data formatting | bytes 5242880 | tf_op jit(solution)/shard_map/concatenate | solution.py:148
  12.3 10.3 %all-to-all-start = ((bf16[128,80,128]{2,1,0:T(8,128)(2,1)}), bf16[128,80,128]{2,1,0:T(8,128)(2,1)S(1)}, u32[]{:S(2)}, u32[]{:S(2)}) async-start(bf16[128,80,128]{2,1,0:T(8,128)(2,1)} %copy.37), calls=%async_computation | async-start | bytes 5242880 | tf_op jit(solution)/shard_map/all_to_all | solution.py:147
  25.8 1.4 compare_reduce_fusion
  28.3 28.5 %all-to-all-done = bf16[128,80,128]{2,1,0:T(8,128)(2,1)S(1)} async-done(((bf16[128,80,128]{2,1,0:T(8,128)(2,1)}), bf16[128,80,128]{2,1,0:T(8,128)(2,1)S(1)}, u32[]{:S(2)}, u32[]{:S(2)}) %all-to-all-start) | async-done | bytes 2621472 | tf_op jit(solution)/shard_map/all_to_all | solution.py:147
  57.0 1.2 copy.46
  58.2 1.2 copy.40
  59.6 4.5 %collective-permute-start.1 = (bf16[128,2176]{1,0:T(8,128)(2,1)S(1)}, bf16[128,2176]{1,0:T(8,128)(2,1)S(1)}, u32[]{:S(2)}, u32[]{:S(2)}) collective-permute-start(bf16[128,2176]{1,0:T(8,128)(2,1)S(1)} %fusion.1.refs_0_), channel_id=1, source_target_pairs={{2,0},{3,1},{4,2},{5,3},{6,4},{7,5},{8,6},{9,7},{10,8},{11,9},{12,... | collective-permute-start | bytes 1671176 | tf_op jit(solution)/shard_map/ppermute | solution.py:19
  64.1 1.9 %collective-permute-start = (bf16[128,2176]{1,0:T(8,128)(2,1)S(1)}, bf16[128,2176]{1,0:T(8,128)(2,1)S(1)}, u32[]{:S(2)}, u32[]{:S(2)}) collective-permute-start(bf16[128,2176]{1,0:T(8,128)(2,1)S(1)} %fusion.1.refs_0_), channel_id=1, source_target_pairs={{0,2},{1,3},{2,4},{3,5},{4,6},{5,7},{6,8},{7,9},{8,10},{9,11},{10,... | collective-permute-start | bytes 1671176 | tf_op jit(solution)/shard_map/ppermute | solution.py:19
  66.8 9.0 %collective-permute-done.1.refs_2_ = bf16[128,2176]{1,0:T(8,128)(2,1)S(1)} collective-permute-done((bf16[128,2176]{1,0:T(8,128)(2,1)S(1)}, bf16[128,2176]{1,0:T(8,128)(2,1)S(1)}, u32[]{:S(2)}, u32[]{:S(2)}) %collective-permute-start.1) | collective-permute-done | bytes 557088 | tf_op jit(solution)/shard_map/ppermute | solution.py:19
  75.9 8.0 %collective-permute-start.3 = (bf16[128,2176]{1,0:T(8,128)(2,1)S(1)}, bf16[128,2176]{1,0:T(8,128)(2,1)S(1)}, u32[]{:S(2)}, u32[]{:S(2)}) collective-permute-start(bf16[128,2176]{1,0:T(8,128)(2,1)S(1)} %collective-permute-done.1.refs_2_), channel_id=1, source_target_pairs={{2,0},{3,1},{4,2},{5,3},{6,4},{7,5},{8,6},{9,7},{10,8},{11,9},{12,... | collective-permute-start | bytes 1671176 | tf_op jit(solution)/shard_map/ppermute | solution.py:19
  83.9 1.9 %collective-permute-start.2 = (bf16[128,2176]{1,0:T(8,128)(2,1)S(1)}, bf16[128,2176]{1,0:T(8,128)(2,1)S(1)}, u32[]{:S(2)}, u32[]{:S(2)}) collective-permute-start(bf16[128,2176]{1,0:T(8,128)(2,1)S(1)} %collective-permute-done.refs_1_), channel_id=1, source_target_pairs={{0,2},{1,3},{2,4},{3,5},{4,6},{5,7},{6,8},{7,9},{8,10},{9,11},{10,... | collective-permute-start | bytes 1671176 | tf_op jit(solution)/shard_map/ppermute | solution.py:19
  87.6 6.8 %collective-permute-done.3.refs_4_ = bf16[128,2176]{1,0:T(8,128)(2,1)S(1)} collective-permute-done((bf16[128,2176]{1,0:T(8,128)(2,1)S(1)}, bf16[128,2176]{1,0:T(8,128)(2,1)S(1)}, u32[]{:S(2)}, u32[]{:S(2)}) %collective-permute-start.3) | collective-permute-done | bytes 557088 | tf_op jit(solution)/shard_map/ppermute | solution.py:19
  94.3 8.6 %collective-permute-start.5 = (bf16[128,2176]{1,0:T(8,128)(2,1)S(1)}, bf16[128,2176]{1,0:T(8,128)(2,1)S(1)}, u32[]{:S(2)}, u32[]{:S(2)}) collective-permute-start(bf16[128,2176]{1,0:T(8,128)(2,1)S(1)} %collective-permute-done.3.refs_4_), channel_id=1, source_target_pairs={{2,0},{3,1},{4,2},{5,3},{6,4},{7,5},{8,6},{9,7},{10,8},{11,9},{12,... | collective-permute-start | bytes 1671176 | tf_op jit(solution)/shard_map/ppermute | solution.py:19
  102.9 1.9 %collective-permute-start.4 = (bf16[128,2176]{1,0:T(8,128)(2,1)S(1)}, bf16[128,2176]{1,0:T(8,128)(2,1)S(1)}, u32[]{:S(2)}, u32[]{:S(2)}) collective-permute-start(bf16[128,2176]{1,0:T(8,128)(2,1)S(1)} %collective-permute-done.2.refs_3_), channel_id=1, source_target_pairs={{0,2},{1,3},{2,4},{3,5},{4,6},{5,7},{6,8},{7,9},{8,10},{9,11},{10,... | collective-permute-start | bytes 1671176 | tf_op jit(solution)/shard_map/ppermute | solution.py:19
  106.6 5.9 %collective-permute-done.5.refs_6_ = bf16[128,2176]{1,0:T(8,128)(2,1)S(1)} collective-permute-done((bf16[128,2176]{1,0:T(8,128)(2,1)S(1)}, bf16[128,2176]{1,0:T(8,128)(2,1)S(1)}, u32[]{:S(2)}, u32[]{:S(2)}) %collective-permute-start.5) | collective-permute-done | bytes 557088 | tf_op jit(solution)/shard_map/ppermute | solution.py:19
  112.5 8.4 %collective-permute-done.4.refs_5_ = bf16[128,2176]{1,0:T(8,128)(2,1)S(1)} collective-permute-done((bf16[128,2176]{1,0:T(8,128)(2,1)S(1)}, bf16[128,2176]{1,0:T(8,128)(2,1)S(1)}, u32[]{:S(2)}, u32[]{:S(2)}) %collective-permute-start.4) | collective-permute-done | bytes 557088 | tf_op jit(solution)/shard_map/ppermute | solution.py:19
  120.9 1.9 %collective-permute-start.6 = (bf16[128,2176]{1,0:T(8,128)(2,1)S(1)}, bf16[128,2176]{1,0:T(8,128)(2,1)S(1)}, u32[]{:S(2)}, u32[]{:S(2)}) collective-permute-start(bf16[128,2176]{1,0:T(8,128)(2,1)S(1)} %broadcast_select_fusion), channel_id=1, source_target_pairs={{1,3},{3,5},{5,7},{7,9},{9,11},{11,13},{13,15},{15,17},{17,19},{19... | collective-permute-start | bytes 1671176 | tf_op jit(solution)/shard_map/ppermute | solution.py:196
  124.5 7.8 %collective-permute-done.6.refs_7_ = bf16[128,2176]{1,0:T(8,128)(2,1)S(1)} collective-permute-done((bf16[128,2176]{1,0:T(8,128)(2,1)S(1)}, bf16[128,2176]{1,0:T(8,128)(2,1)S(1)}, u32[]{:S(2)}, u32[]{:S(2)}) %collective-permute-start.6) | collective-permute-done | bytes 557088 | tf_op jit(solution)/shard_map/ppermute | solution.py:196
  133.7 1.4 copy.48
  135.1 3.0 %copy.45.q_ref = bf16[32,128,256]{2,1,0:T(8,128)(2,1)} copy(bf16[32,128,256]{1,2,0:T(8,128)(2,1)S(1)} %bitcast.43) | data formatting | bytes 4194304 | tf_op jit(solution)/shard_map/reshape | solution.py:182
  138.1 3.2 %collective-permute-done.7.stack_ref = bf16[8,128,2176]{2,1,0:T(8,128)(2,1)} collective-permute-done((bf16[8,128,2176]{2,1,0:T(8,128)(2,1)}, bf16[8,128,2176]{2,1,0:T(8,128)(2,1)}, u32[]{:S(2)}, u32[]{:S(2)}) %collective-permute-start.7) | collective-permute-done | bytes 4456480 | tf_op jit(solution)/shard_map/ppermute | solution.py:197
  141.3 42.1 %shard_map.86 = (bf16[128,8192]{1,0:T(8,128)(2,1)}, f32[128,128]{1,0:T(8,128)}) custom-call(s32[17]{0:T(128)} %pad_add_fusion.1.meta_ref, bf16[32,128,256]{2,1,0:T(8,128)(2,1)} %copy.45.q_ref, bf16[8,128,2176]{2,1,0:T(8,128)(2,1)} %collective-permute-done.7.stack_ref, bf16[128,2176]{1,0:T(8,128)(2,1)} %copy-done.3, bf16[128,2176]{1,0:T(8,128)(2,1)} %copy-done.5, ...), custom_call_target="tpu_custom_call" | custom-call | tf_op jit(solution)/shard_map/pallas_call | solution.py:117
  (62 shorter events, 15.9 us)
Async XLA Ops:
  0.6 183.7 %copy-start = (bf16[8192,16]{0,1:T(8,128)(2,1)S(1)}, bf16[8192,16]{0,1:T(8,128)(2,1)}, u32[]{:S(2)}) copy-start(bf16[8192,16]{0,1:T(8,128)(2,1)} %param.13) | copy-start | bytes 786436
  8.9 13.7 %copy-start.9 = (s32[32]{0:T(128)S(1)}, s32[32]{0:T(128)}, u32[]{:S(2)}) copy-start(s32[32]{0:T(128)} %param.12) | copy-start | bytes 388
  8.9 14.7 %copy-start.10 = (s32[8]{0:T(128)S(1)}, s32[8]{0:T(128)}, u32[]{:S(2)}) copy-start(s32[8]{0:T(128)} %constant.85.clone) | copy-start | bytes 100
  9.0 14.7 %copy-start.11 = (s32[8]{0:T(128)S(1)}, s32[8]{0:T(128)}, u32[]{:S(2)}) copy-start(s32[8]{0:T(128)} %constant.84.clone) | copy-start | bytes 100
  12.3 44.6 %all-to-all-start = ((bf16[128,80,128]{2,1,0:T(8,128)(2,1)}), bf16[128,80,128]{2,1,0:T(8,128)(2,1)S(1)}, u32[]{:S(2)}, u32[]{:S(2)}) async-start(bf16[128,80,128]{2,1,0:T(8,128)(2,1)} %copy.37), calls=%async_computation | async-start | bytes 5242880 | tf_op jit(solution)/shard_map/all_to_all | solution.py:147
  59.5 43.4 %copy-start.3 = (bf16[128,2176]{1,0:T(8,128)(2,1)}, bf16[128,2176]{1,0:T(8,128)(2,1)S(1)}, u32[]{:S(2)}) copy-start(bf16[128,2176]{1,0:T(8,128)(2,1)S(1)} %fusion.1.refs_0_) | copy-start | bytes 1671172
  59.6 16.3 %collective-permute-start.1 = (bf16[128,2176]{1,0:T(8,128)(2,1)S(1)}, bf16[128,2176]{1,0:T(8,128)(2,1)S(1)}, u32[]{:S(2)}, u32[]{:S(2)}) collective-permute-start(bf16[128,2176]{1,0:T(8,128)(2,1)S(1)} %fusion.1.refs_0_), channel_id=1, source_target_pairs={{2,0},{3,1},{4,2},{5,3},{6,4},{7,5},{8,6},{9,7},{10,8},{11,9},{12,... | collective-permute-start | bytes 1671176 | tf_op jit(solution)/shard_map/ppermute | solution.py:19
  64.1 19.9 %collective-permute-start = (bf16[128,2176]{1,0:T(8,128)(2,1)S(1)}, bf16[128,2176]{1,0:T(8,128)(2,1)S(1)}, u32[]{:S(2)}, u32[]{:S(2)}) collective-permute-start(bf16[128,2176]{1,0:T(8,128)(2,1)S(1)} %fusion.1.refs_0_), channel_id=1, source_target_pairs={{0,2},{1,3},{2,4},{3,5},{4,6},{5,7},{6,8},{7,9},{8,10},{9,11},{10,... | collective-permute-start | bytes 1671176 | tf_op jit(solution)/shard_map/ppermute | solution.py:19
  75.9 57.4 %copy-start.4 = (bf16[128,2176]{1,0:T(8,128)(2,1)}, bf16[128,2176]{1,0:T(8,128)(2,1)S(1)}, u32[]{:S(2)}) copy-start(bf16[128,2176]{1,0:T(8,128)(2,1)S(1)} %collective-permute-done.1.refs_2_) | copy-start | bytes 1671172
  75.9 18.4 %collective-permute-start.3 = (bf16[128,2176]{1,0:T(8,128)(2,1)S(1)}, bf16[128,2176]{1,0:T(8,128)(2,1)S(1)}, u32[]{:S(2)}, u32[]{:S(2)}) collective-permute-start(bf16[128,2176]{1,0:T(8,128)(2,1)S(1)} %collective-permute-done.1.refs_2_), channel_id=1, source_target_pairs={{2,0},{3,1},{4,2},{5,3},{6,4},{7,5},{8,6},{9,7},{10,8},{11,9},{12,... | collective-permute-start | bytes 1671176 | tf_op jit(solution)/shard_map/ppermute | solution.py:19
  83.9 49.4 %copy-start.5 = (bf16[128,2176]{1,0:T(8,128)(2,1)}, bf16[128,2176]{1,0:T(8,128)(2,1)S(1)}, u32[]{:S(2)}) copy-start(bf16[128,2176]{1,0:T(8,128)(2,1)S(1)} %collective-permute-done.refs_1_) | copy-start | bytes 1671172
  83.9 19.0 %collective-permute-start.2 = (bf16[128,2176]{1,0:T(8,128)(2,1)S(1)}, bf16[128,2176]{1,0:T(8,128)(2,1)S(1)}, u32[]{:S(2)}, u32[]{:S(2)}) collective-permute-start(bf16[128,2176]{1,0:T(8,128)(2,1)S(1)} %collective-permute-done.refs_1_), channel_id=1, source_target_pairs={{0,2},{1,3},{2,4},{3,5},{4,6},{5,7},{6,8},{7,9},{8,10},{9,11},{10,... | collective-permute-start | bytes 1671176 | tf_op jit(solution)/shard_map/ppermute | solution.py:19
  94.3 39.0 %copy-start.6 = (bf16[128,2176]{1,0:T(8,128)(2,1)}, bf16[128,2176]{1,0:T(8,128)(2,1)S(1)}, u32[]{:S(2)}) copy-start(bf16[128,2176]{1,0:T(8,128)(2,1)S(1)} %collective-permute-done.3.refs_4_) | copy-start | bytes 1671172
  94.3 18.1 %collective-permute-start.5 = (bf16[128,2176]{1,0:T(8,128)(2,1)S(1)}, bf16[128,2176]{1,0:T(8,128)(2,1)S(1)}, u32[]{:S(2)}, u32[]{:S(2)}) collective-permute-start(bf16[128,2176]{1,0:T(8,128)(2,1)S(1)} %collective-permute-done.3.refs_4_), channel_id=1, source_target_pairs={{2,0},{3,1},{4,2},{5,3},{6,4},{7,5},{8,6},{9,7},{10,8},{11,9},{12,... | collective-permute-start | bytes 1671176 | tf_op jit(solution)/shard_map/ppermute | solution.py:19
  102.9 30.4 %copy-start.7 = (bf16[128,2176]{1,0:T(8,128)(2,1)}, bf16[128,2176]{1,0:T(8,128)(2,1)S(1)}, u32[]{:S(2)}) copy-start(bf16[128,2176]{1,0:T(8,128)(2,1)S(1)} %collective-permute-done.2.refs_3_) | copy-start | bytes 1671172
  102.9 17.9 %collective-permute-start.4 = (bf16[128,2176]{1,0:T(8,128)(2,1)S(1)}, bf16[128,2176]{1,0:T(8,128)(2,1)S(1)}, u32[]{:S(2)}, u32[]{:S(2)}) collective-permute-start(bf16[128,2176]{1,0:T(8,128)(2,1)S(1)} %collective-permute-done.2.refs_3_), channel_id=1, source_target_pairs={{0,2},{1,3},{2,4},{3,5},{4,6},{5,7},{6,8},{7,9},{8,10},{9,11},{10,... | collective-permute-start | bytes 1671176 | tf_op jit(solution)/shard_map/ppermute | solution.py:19
  112.5 21.2 %copy-start.1 = (bf16[128,2176]{1,0:T(8,128)(2,1)}, bf16[128,2176]{1,0:T(8,128)(2,1)S(1)}, u32[]{:S(2)}) copy-start(bf16[128,2176]{1,0:T(8,128)(2,1)S(1)} %collective-permute-done.5.refs_6_) | copy-start | bytes 1671172
  120.8 12.5 %copy-start.2 = (bf16[128,2176]{1,0:T(8,128)(2,1)}, bf16[128,2176]{1,0:T(8,128)(2,1)S(1)}, u32[]{:S(2)}) copy-start(bf16[128,2176]{1,0:T(8,128)(2,1)S(1)} %collective-permute-done.4.refs_5_) | copy-start | bytes 1671172
  120.9 11.4 %collective-permute-start.6 = (bf16[128,2176]{1,0:T(8,128)(2,1)S(1)}, bf16[128,2176]{1,0:T(8,128)(2,1)S(1)}, u32[]{:S(2)}, u32[]{:S(2)}) collective-permute-start(bf16[128,2176]{1,0:T(8,128)(2,1)S(1)} %broadcast_select_fusion), channel_id=1, source_target_pairs={{1,3},{3,5},{5,7},{7,9},{9,11},{11,13},{13,15},{15,17},{17,19},{19... | collective-permute-start | bytes 1671176 | tf_op jit(solution)/shard_map/ppermute | solution.py:196
  132.3 1.1 copy-start.8
  133.4 7.9 %collective-permute-start.7 = (bf16[8,128,2176]{2,1,0:T(8,128)(2,1)}, bf16[8,128,2176]{2,1,0:T(8,128)(2,1)}, u32[]{:S(2)}, u32[]{:S(2)}) collective-permute-start(bf16[8,128,2176]{2,1,0:T(8,128)(2,1)} %bitcast_dynamic-update-slice_fusion), channel_id=1, source_target_pairs={{0,1},{1,0},{2,3},{3,2},{4,5},{5,4},{6,7},{7,6},{8,9},{9,8},{10,11... | collective-permute-start | bytes 13369352 | tf_op jit(solution)/shard_map/ppermute | solution.py:197

commit v2 on v0

--- a/solution.py
+++ b/solution.py
@@ -92,7 +92,7 @@
             merge(first, m0_ref, l0_ref, acc0_ref, 0, *scored(k, vt, q0t), mask=column_head == h)
             return carry
 
-        lax.fori_loop(0, heads_kv, one_head, 0)
+        lax.fori_loop(0, heads_kv, one_head, 0, unroll=2)
 
     tile_step(loaders[0], True)
     for t in range(1, tiles):

time: 185 us -> 177 us (0.957)
  the two profiles are of different devices: /device:TPU:25 before, /device:TPU:9 now
where the time goes in v2:
time: 177 us
  waiting for transfers between devices  69.6 us (39%)
  starting transfers between devices  39.3 us (22%)
  Pallas kernels  33.6 us (19%)
  local copies, waits for them, and re-layouts  26.9 us (15%)
  other arithmetic  5.72 us (3%)
    pallas_call x1, Pallas kernels, attend(): pl.pallas_call(attention_kernel, out_shape=(jax.ShapeDtypeStruct((rows, h...  33.6 us
    all_to_all x1, waiting for transfers between devices, shards(): lax.all_to_all(jnp.concatenate([queries.reshape(devices, heads, DH), keys...  28.9 us
    ppermute x6, waiting for transfers between devices, shifted(): return lax.ppermute(block, axis, route)  27 us
    ppermute x6, starting transfers between devices, shifted(): return lax.ppermute(block, axis, route)  25.2 us
    unnamed x37, local copies, waits for them, and re-layouts  15.2 us
    ppermute x1, waiting for transfers between devices, shards(): pieces.append(lax.ppermute(onward, 'seq', route))  10.9 us
    all_to_all x1, starting transfers between devices, shards(): lax.all_to_all(jnp.concatenate([queries.reshape(devices, heads, DH), keys...  10.7 us
  transfers between devices with their start and end apart: 9, of which 7 were waited for; matrix products, arithmetic and copies ran while one was open for 9% of the time, Pallas kernels for 0%

profile of v2, /device:TPU:9, one launch (start us, length us, event | category | flops | bytes accessed | tf_op | source)
XLA Modules:
  0.0 176.8 jit_solution(3718327538250096790)
XLA Ops:
  2.9 4.1 %copy.34 = bf16[128,8192]{0,1:T(8,128)(2,1)} copy(bf16[128,8192]{1,0:T(8,128)(2,1)} %param.9) | data formatting | bytes 4194304 | tf_op args[0]
  7.0 1.9 %pad_maximum_fusion = bf16[128,80,128]{0,2,1:T(8,128)(2,1)S(1)} fusion(bf16[128,8,128]{0,2,1:T(8,128)(2,1)S(1)} %bitcast.46, bf16[128,8,128]{0,2,1:T(8,128)(2,1)S(1)} %bitcast.45, bf16[128,64,128]{0,2,1:T(8,128)(2,1)} %bitcast.42), kind=kLoop, calls=%fused_computation.1 | loop fusion | flops 2621440 | bytes 5242880 | tf_op jit(solution)/shard_map/concatenate | solution.py:148
  9.0 3.3 %copy.37 = bf16[128,80,128]{2,1,0:T(8,128)(2,1)} copy(bf16[128,80,128]{0,2,1:T(8,128)(2,1)S(1)} %pad_maximum_fusion) | data formatting | bytes 5242880 | tf_op jit(solution)/shard_map/concatenate | solution.py:148
  12.3 10.7 %all-to-all-start = ((bf16[128,80,128]{2,1,0:T(8,128)(2,1)}), bf16[128,80,128]{2,1,0:T(8,128)(2,1)S(1)}, u32[]{:S(2)}, u32[]{:S(2)}) async-start(bf16[128,80,128]{2,1,0:T(8,128)(2,1)} %copy.37), calls=%async_computation | async-start | bytes 5242880 | tf_op jit(solution)/shard_map/all_to_all | solution.py:147
  26.2 1.4 compare_reduce_fusion
  28.7 28.9 %all-to-all-done = bf16[128,80,128]{2,1,0:T(8,128)(2,1)S(1)} async-done(((bf16[128,80,128]{2,1,0:T(8,128)(2,1)}), bf16[128,80,128]{2,1,0:T(8,128)(2,1)S(1)}, u32[]{:S(2)}, u32[]{:S(2)}) %all-to-all-start) | async-done | bytes 2621472 | tf_op jit(solution)/shard_map/all_to_all | solution.py:147
  59.0 1.2 copy.40
  60.3 3.6 %collective-permute-start.1 = (bf16[128,2176]{1,0:T(8,128)(2,1)S(1)}, bf16[128,2176]{1,0:T(8,128)(2,1)S(1)}, u32[]{:S(2)}, u32[]{:S(2)}) collective-permute-start(bf16[128,2176]{1,0:T(8,128)(2,1)S(1)} %fusion.1.refs_0_), channel_id=1, source_target_pairs={{2,0},{3,1},{4,2},{5,3},{6,4},{7,5},{8,6},{9,7},{10,8},{11,9},{12,... | collective-permute-start | bytes 1671176 | tf_op jit(solution)/shard_map/ppermute | solution.py:19
  63.9 1.9 %collective-permute-start = (bf16[128,2176]{1,0:T(8,128)(2,1)S(1)}, bf16[128,2176]{1,0:T(8,128)(2,1)S(1)}, u32[]{:S(2)}, u32[]{:S(2)}) collective-permute-start(bf16[128,2176]{1,0:T(8,128)(2,1)S(1)} %fusion.1.refs_0_), channel_id=1, source_target_pairs={{0,2},{1,3},{2,4},{3,5},{4,6},{5,7},{6,8},{7,9},{8,10},{9,11},{10,... | collective-permute-start | bytes 1671176 | tf_op jit(solution)/shard_map/ppermute | solution.py:19
  66.7 8.2 %collective-permute-done.1.refs_2_ = bf16[128,2176]{1,0:T(8,128)(2,1)S(1)} collective-permute-done((bf16[128,2176]{1,0:T(8,128)(2,1)S(1)}, bf16[128,2176]{1,0:T(8,128)(2,1)S(1)}, u32[]{:S(2)}, u32[]{:S(2)}) %collective-permute-start.1) | collective-permute-done | bytes 557088 | tf_op jit(solution)/shard_map/ppermute | solution.py:19
  74.9 7.6 %collective-permute-start.3 = (bf16[128,2176]{1,0:T(8,128)(2,1)S(1)}, bf16[128,2176]{1,0:T(8,128)(2,1)S(1)}, u32[]{:S(2)}, u32[]{:S(2)}) collective-permute-start(bf16[128,2176]{1,0:T(8,128)(2,1)S(1)} %collective-permute-done.1.refs_2_), channel_id=1, source_target_pairs={{2,0},{3,1},{4,2},{5,3},{6,4},{7,5},{8,6},{9,7},{10,8},{11,9},{12,... | collective-permute-start | bytes 1671176 | tf_op jit(solution)/shard_map/ppermute | solution.py:19
  82.5 1.9 %collective-permute-start.2 = (bf16[128,2176]{1,0:T(8,128)(2,1)S(1)}, bf16[128,2176]{1,0:T(8,128)(2,1)S(1)}, u32[]{:S(2)}, u32[]{:S(2)}) collective-permute-start(bf16[128,2176]{1,0:T(8,128)(2,1)S(1)} %collective-permute-done.refs_1_), channel_id=1, source_target_pairs={{0,2},{1,3},{2,4},{3,5},{4,6},{5,7},{6,8},{7,9},{8,10},{9,11},{10,... | collective-permute-start | bytes 1671176 | tf_op jit(solution)/shard_map/ppermute | solution.py:19
  86.2 5.8 %collective-permute-done.3.refs_4_ = bf16[128,2176]{1,0:T(8,128)(2,1)S(1)} collective-permute-done((bf16[128,2176]{1,0:T(8,128)(2,1)S(1)}, bf16[128,2176]{1,0:T(8,128)(2,1)S(1)}, u32[]{:S(2)}, u32[]{:S(2)}) %collective-permute-start.3) | collective-permute-done | bytes 557088 | tf_op jit(solution)/shard_map/ppermute | solution.py:19
  91.9 8.3 %collective-permute-start.5 = (bf16[128,2176]{1,0:T(8,128)(2,1)S(1)}, bf16[128,2176]{1,0:T(8,128)(2,1)S(1)}, u32[]{:S(2)}, u32[]{:S(2)}) collective-permute-start(bf16[128,2176]{1,0:T(8,128)(2,1)S(1)} %collective-permute-done.3.refs_4_), channel_id=1, source_target_pairs={{2,0},{3,1},{4,2},{5,3},{6,4},{7,5},{8,6},{9,7},{10,8},{11,9},{12,... | collective-permute-start | bytes 1671176 | tf_op jit(solution)/shard_map/ppermute | solution.py:19
  100.3 1.9 %collective-permute-start.4 = (bf16[128,2176]{1,0:T(8,128)(2,1)S(1)}, bf16[128,2176]{1,0:T(8,128)(2,1)S(1)}, u32[]{:S(2)}, u32[]{:S(2)}) collective-permute-start(bf16[128,2176]{1,0:T(8,128)(2,1)S(1)} %collective-permute-done.2.refs_3_), channel_id=1, source_target_pairs={{0,2},{1,3},{2,4},{3,5},{4,6},{5,7},{6,8},{7,9},{8,10},{9,11},{10,... | collective-permute-start | bytes 1671176 | tf_op jit(solution)/shard_map/ppermute | solution.py:19
  103.9 4.9 %collective-permute-done.5.refs_6_ = bf16[128,2176]{1,0:T(8,128)(2,1)S(1)} collective-permute-done((bf16[128,2176]{1,0:T(8,128)(2,1)S(1)}, bf16[128,2176]{1,0:T(8,128)(2,1)S(1)}, u32[]{:S(2)}, u32[]{:S(2)}) %collective-permute-start.5) | collective-permute-done | bytes 557088 | tf_op jit(solution)/shard_map/ppermute | solution.py:19
  108.8 8.1 %collective-permute-done.4.refs_5_ = bf16[128,2176]{1,0:T(8,128)(2,1)S(1)} collective-permute-done((bf16[128,2176]{1,0:T(8,128)(2,1)S(1)}, bf16[128,2176]{1,0:T(8,128)(2,1)S(1)}, u32[]{:S(2)}, u32[]{:S(2)}) %collective-permute-start.4) | collective-permute-done | bytes 557088 | tf_op jit(solution)/shard_map/ppermute | solution.py:19
  117.0 1.9 %collective-permute-start.6 = (bf16[128,2176]{1,0:T(8,128)(2,1)S(1)}, bf16[128,2176]{1,0:T(8,128)(2,1)S(1)}, u32[]{:S(2)}, u32[]{:S(2)}) collective-permute-start(bf16[128,2176]{1,0:T(8,128)(2,1)S(1)} %broadcast_select_fusion), channel_id=1, source_target_pairs={{1,3},{3,5},{5,7},{7,9},{9,11},{11,13},{13,15},{15,17},{17,19},{19... | collective-permute-start | bytes 1671176 | tf_op jit(solution)/shard_map/ppermute | solution.py:196
  120.6 10.9 %collective-permute-done.6.refs_7_ = bf16[128,2176]{1,0:T(8,128)(2,1)S(1)} collective-permute-done((bf16[128,2176]{1,0:T(8,128)(2,1)S(1)}, bf16[128,2176]{1,0:T(8,128)(2,1)S(1)}, u32[]{:S(2)}, u32[]{:S(2)}) %collective-permute-start.6) | collective-permute-done | bytes 557088 | tf_op jit(solution)/shard_map/ppermute | solution.py:196
  132.6 1.5 collective-permute-start.7
  134.3 1.4 copy.48
  135.7 3.0 %copy.45.q_ref = bf16[32,128,256]{2,1,0:T(8,128)(2,1)} copy(bf16[32,128,256]{1,2,0:T(8,128)(2,1)S(1)} %bitcast.43) | data formatting | bytes 4194304 | tf_op jit(solution)/shard_map/reshape | solution.py:182
  138.7 2.8 %collective-permute-done.7.stack_ref = bf16[8,128,2176]{2,1,0:T(8,128)(2,1)} collective-permute-done((bf16[8,128,2176]{2,1,0:T(8,128)(2,1)}, bf16[8,128,2176]{2,1,0:T(8,128)(2,1)}, u32[]{:S(2)}, u32[]{:S(2)}) %collective-permute-start.7) | collective-permute-done | bytes 4456480 | tf_op jit(solution)/shard_map/ppermute | solution.py:197
  141.5 33.6 %shard_map.86 = (bf16[128,8192]{1,0:T(8,128)(2,1)}, f32[128,128]{1,0:T(8,128)}) custom-call(s32[17]{0:T(128)} %pad_add_fusion.1.meta_ref, bf16[32,128,256]{2,1,0:T(8,128)(2,1)} %copy.45.q_ref, bf16[8,128,2176]{2,1,0:T(8,128)(2,1)} %collective-permute-done.7.stack_ref, bf16[128,2176]{1,0:T(8,128)(2,1)} %copy-done.3, bf16[128,2176]{1,0:T(8,128)(2,1)} %copy-done.5, ...), custom_call_target="tpu_custom_call" | custom-call | tf_op jit(solution)/shard_map/pallas_call | solution.py:117
  (62 shorter events, 17.1 us)
Async XLA Ops:
  0.6 175.5 %copy-start = (bf16[8192,16]{0,1:T(8,128)(2,1)S(1)}, bf16[8192,16]{0,1:T(8,128)(2,1)}, u32[]{:S(2)}) copy-start(bf16[8192,16]{0,1:T(8,128)(2,1)} %param.13) | copy-start | bytes 786436
  8.9 14.1 %copy-start.9 = (s32[32]{0:T(128)S(1)}, s32[32]{0:T(128)}, u32[]{:S(2)}) copy-start(s32[32]{0:T(128)} %param.12) | copy-start | bytes 388
  8.9 15.1 %copy-start.10 = (s32[8]{0:T(128)S(1)}, s32[8]{0:T(128)}, u32[]{:S(2)}) copy-start(s32[8]{0:T(128)} %constant.85.clone) | copy-start | bytes 100
  9.0 15.1 %copy-start.11 = (s32[8]{0:T(128)S(1)}, s32[8]{0:T(128)}, u32[]{:S(2)}) copy-start(s32[8]{0:T(128)} %constant.84.clone) | copy-start | bytes 100
  12.3 45.3 %all-to-all-start = ((bf16[128,80,128]{2,1,0:T(8,128)(2,1)}), bf16[128,80,128]{2,1,0:T(8,128)(2,1)S(1)}, u32[]{:S(2)}, u32[]{:S(2)}) async-start(bf16[128,80,128]{2,1,0:T(8,128)(2,1)} %copy.37), calls=%async_computation | async-start | bytes 5242880 | tf_op jit(solution)/shard_map/all_to_all | solution.py:147
  60.3 39.9 %copy-start.3 = (bf16[128,2176]{1,0:T(8,128)(2,1)}, bf16[128,2176]{1,0:T(8,128)(2,1)S(1)}, u32[]{:S(2)}) copy-start(bf16[128,2176]{1,0:T(8,128)(2,1)S(1)} %fusion.1.refs_0_) | copy-start | bytes 1671172
  60.3 14.6 %collective-permute-start.1 = (bf16[128,2176]{1,0:T(8,128)(2,1)S(1)}, bf16[128,2176]{1,0:T(8,128)(2,1)S(1)}, u32[]{:S(2)}, u32[]{:S(2)}) collective-permute-start(bf16[128,2176]{1,0:T(8,128)(2,1)S(1)} %fusion.1.refs_0_), channel_id=1, source_target_pairs={{2,0},{3,1},{4,2},{5,3},{6,4},{7,5},{8,6},{9,7},{10,8},{11,9},{12,... | collective-permute-start | bytes 1671176 | tf_op jit(solution)/shard_map/ppermute | solution.py:19
  63.9 18.6 %collective-permute-start = (bf16[128,2176]{1,0:T(8,128)(2,1)S(1)}, bf16[128,2176]{1,0:T(8,128)(2,1)S(1)}, u32[]{:S(2)}, u32[]{:S(2)}) collective-permute-start(bf16[128,2176]{1,0:T(8,128)(2,1)S(1)} %fusion.1.refs_0_), channel_id=1, source_target_pairs={{0,2},{1,3},{2,4},{3,5},{4,6},{5,7},{6,8},{7,9},{8,10},{9,11},{10,... | collective-permute-start | bytes 1671176 | tf_op jit(solution)/shard_map/ppermute | solution.py:19
  74.9 57.5 %copy-start.4 = (bf16[128,2176]{1,0:T(8,128)(2,1)}, bf16[128,2176]{1,0:T(8,128)(2,1)S(1)}, u32[]{:S(2)}) copy-start(bf16[128,2176]{1,0:T(8,128)(2,1)S(1)} %collective-permute-done.1.refs_2_) | copy-start | bytes 1671172
  74.9 17.0 %collective-permute-start.3 = (bf16[128,2176]{1,0:T(8,128)(2,1)S(1)}, bf16[128,2176]{1,0:T(8,128)(2,1)S(1)}, u32[]{:S(2)}, u32[]{:S(2)}) collective-permute-start(bf16[128,2176]{1,0:T(8,128)(2,1)S(1)} %collective-permute-done.1.refs_2_), channel_id=1, source_target_pairs={{2,0},{3,1},{4,2},{5,3},{6,4},{7,5},{8,6},{9,7},{10,8},{11,9},{12,... | collective-permute-start | bytes 1671176 | tf_op jit(solution)/shard_map/ppermute | solution.py:19
  82.5 49.9 %copy-start.5 = (bf16[128,2176]{1,0:T(8,128)(2,1)}, bf16[128,2176]{1,0:T(8,128)(2,1)S(1)}, u32[]{:S(2)}) copy-start(bf16[128,2176]{1,0:T(8,128)(2,1)S(1)} %collective-permute-done.refs_1_) | copy-start | bytes 1671172
  82.5 17.7 %collective-permute-start.2 = (bf16[128,2176]{1,0:T(8,128)(2,1)S(1)}, bf16[128,2176]{1,0:T(8,128)(2,1)S(1)}, u32[]{:S(2)}, u32[]{:S(2)}) collective-permute-start(bf16[128,2176]{1,0:T(8,128)(2,1)S(1)} %collective-permute-done.refs_1_), channel_id=1, source_target_pairs={{0,2},{1,3},{2,4},{3,5},{4,6},{5,7},{6,8},{7,9},{8,10},{9,11},{10,... | collective-permute-start | bytes 1671176 | tf_op jit(solution)/shard_map/ppermute | solution.py:19
  91.9 40.5 %copy-start.6 = (bf16[128,2176]{1,0:T(8,128)(2,1)}, bf16[128,2176]{1,0:T(8,128)(2,1)S(1)}, u32[]{:S(2)}) copy-start(bf16[128,2176]{1,0:T(8,128)(2,1)S(1)} %collective-permute-done.3.refs_4_) | copy-start | bytes 1671172
  91.9 16.9 %collective-permute-start.5 = (bf16[128,2176]{1,0:T(8,128)(2,1)S(1)}, bf16[128,2176]{1,0:T(8,128)(2,1)S(1)}, u32[]{:S(2)}, u32[]{:S(2)}) collective-permute-start(bf16[128,2176]{1,0:T(8,128)(2,1)S(1)} %collective-permute-done.3.refs_4_), channel_id=1, source_target_pairs={{2,0},{3,1},{4,2},{5,3},{6,4},{7,5},{8,6},{9,7},{10,8},{11,9},{12,... | collective-permute-start | bytes 1671176 | tf_op jit(solution)/shard_map/ppermute | solution.py:19
  100.3 32.2 %copy-start.7 = (bf16[128,2176]{1,0:T(8,128)(2,1)}, bf16[128,2176]{1,0:T(8,128)(2,1)S(1)}, u32[]{:S(2)}) copy-start(bf16[128,2176]{1,0:T(8,128)(2,1)S(1)} %collective-permute-done.2.refs_3_) | copy-start | bytes 1671172
  100.3 16.6 %collective-permute-start.4 = (bf16[128,2176]{1,0:T(8,128)(2,1)S(1)}, bf16[128,2176]{1,0:T(8,128)(2,1)S(1)}, u32[]{:S(2)}, u32[]{:S(2)}) collective-permute-start(bf16[128,2176]{1,0:T(8,128)(2,1)S(1)} %collective-permute-done.2.refs_3_), channel_id=1, source_target_pairs={{0,2},{1,3},{2,4},{3,5},{4,6},{5,7},{6,8},{7,9},{8,10},{9,11},{10,... | collective-permute-start | bytes 1671176 | tf_op jit(solution)/shard_map/ppermute | solution.py:19
  108.8 25.5 %copy-start.1 = (bf16[128,2176]{1,0:T(8,128)(2,1)}, bf16[128,2176]{1,0:T(8,128)(2,1)S(1)}, u32[]{:S(2)}) copy-start(bf16[128,2176]{1,0:T(8,128)(2,1)S(1)} %collective-permute-done.5.refs_6_) | copy-start | bytes 1671172
  116.9 15.5 %copy-start.2 = (bf16[128,2176]{1,0:T(8,128)(2,1)}, bf16[128,2176]{1,0:T(8,128)(2,1)S(1)}, u32[]{:S(2)}) copy-start(bf16[128,2176]{1,0:T(8,128)(2,1)S(1)} %collective-permute-done.4.refs_5_) | copy-start | bytes 1671172
  117.0 14.5 %collective-permute-start.6 = (bf16[128,2176]{1,0:T(8,128)(2,1)S(1)}, bf16[128,2176]{1,0:T(8,128)(2,1)S(1)}, u32[]{:S(2)}, u32[]{:S(2)}) collective-permute-start(bf16[128,2176]{1,0:T(8,128)(2,1)S(1)} %broadcast_select_fusion), channel_id=1, source_target_pairs={{1,3},{3,5},{5,7},{7,9},{9,11},{11,13},{13,15},{15,17},{17,19},{19... | collective-permute-start | bytes 1671176 | tf_op jit(solution)/shard_map/ppermute | solution.py:196
  131.5 1.1 copy-start.8
  132.6 9.0 %collective-permute-start.7 = (bf16[8,128,2176]{2,1,0:T(8,128)(2,1)}, bf16[8,128,2176]{2,1,0:T(8,128)(2,1)}, u32[]{:S(2)}, u32[]{:S(2)}) collective-permute-start(bf16[8,128,2176]{2,1,0:T(8,128)(2,1)} %bitcast_dynamic-update-slice_fusion), channel_id=1, source_target_pairs={{0,1},{1,0},{2,3},{3,2},{4,5},{5,4},{6,7},{7,6},{8,9},{9,8},{10,11... | collective-permute-start | bytes 13369352 | tf_op jit(solution)/shard_map/ppermute | solution.py:197

commit v3 on v2

--- a/solution.py
+++ b/solution.py
@@ -107,7 +107,7 @@
         out_ref[:, pl.ds(pl.multiple_of((2 * j + 1) * DH, DH), DH)] = normed[rows:]
         return carry
 
-    lax.fori_loop(0, heads // 2, finish, 0)
+    lax.fori_loop(0, heads // 2, finish, 0, unroll=2)
     out0_ref[...] = acc0_ref[0] / l0_ref[0]
 
 

time: 177 us -> 176 us (level)
  no operation moved by 1% of the time
where the time goes in v3:
time: 176 us; the launch traced here: 175 us
  waiting for transfers between devices  69.6 us (40%)
  starting transfers between devices  39.4 us (22%)
  Pallas kernels  31.9 us (18%)
  local copies, waits for them, and re-layouts  26.9 us (15%)
  other arithmetic  5.72 us (3%)
    pallas_call x1, Pallas kernels, attend(): pl.pallas_call(attention_kernel, out_shape=(jax.ShapeDtypeStruct((rows, h...  31.9 us
    all_to_all x1, waiting for transfers between devices, shards(): lax.all_to_all(jnp.concatenate([queries.reshape(devices, heads, DH), keys...  28.9 us
    ppermute x6, waiting for transfers between devices, shifted(): return lax.ppermute(block, axis, route)  27 us
    ppermute x6, starting transfers between devices, shifted(): return lax.ppermute(block, axis, route)  25.2 us
    unnamed x37, local copies, waits for them, and re-layouts  15.2 us
    ppermute x1, waiting for transfers between devices, shards(): pieces.append(lax.ppermute(onward, 'seq', route))  10.9 us
    all_to_all x1, starting transfers between devices, shards(): lax.all_to_all(jnp.concatenate([queries.reshape(devices, heads, DH), keys...  10.7 us
  transfers between devices with their start and end apart: 9, of which 7 were waited for; matrix products, arithmetic and copies ran while one was open for 9% of the time, Pallas kernels for 0%

profile of v3, /device:TPU:9, one launch (start us, length us, event | category | flops | bytes accessed | tf_op | source)
XLA Modules:
  0.0 175.1 jit_solution(14963872706445502375)
XLA Ops:
  2.9 4.1 %copy.34 = bf16[128,8192]{0,1:T(8,128)(2,1)} copy(bf16[128,8192]{1,0:T(8,128)(2,1)} %param.9) | data formatting | bytes 4194304 | tf_op args[0]
  7.0 1.9 %pad_maximum_fusion = bf16[128,80,128]{0,2,1:T(8,128)(2,1)S(1)} fusion(bf16[128,8,128]{0,2,1:T(8,128)(2,1)S(1)} %bitcast.46, bf16[128,8,128]{0,2,1:T(8,128)(2,1)S(1)} %bitcast.45, bf16[128,64,128]{0,2,1:T(8,128)(2,1)} %bitcast.42), kind=kLoop, calls=%fused_computation.1 | loop fusion | flops 2621440 | bytes 5242880 | tf_op jit(solution)/shard_map/concatenate | solution.py:148
  9.0 3.3 %copy.37 = bf16[128,80,128]{2,1,0:T(8,128)(2,1)} copy(bf16[128,80,128]{0,2,1:T(8,128)(2,1)S(1)} %pad_maximum_fusion) | data formatting | bytes 5242880 | tf_op jit(solution)/shard_map/concatenate | solution.py:148
  12.3 10.7 %all-to-all-start = ((bf16[128,80,128]{2,1,0:T(8,128)(2,1)}), bf16[128,80,128]{2,1,0:T(8,128)(2,1)S(1)}, u32[]{:S(2)}, u32[]{:S(2)}) async-start(bf16[128,80,128]{2,1,0:T(8,128)(2,1)} %copy.37), calls=%async_computation | async-start | bytes 5242880 | tf_op jit(solution)/shard_map/all_to_all | solution.py:147
  26.2 1.4 compare_reduce_fusion
  28.7 28.9 %all-to-all-done = bf16[128,80,128]{2,1,0:T(8,128)(2,1)S(1)} async-done(((bf16[128,80,128]{2,1,0:T(8,128)(2,1)}), bf16[128,80,128]{2,1,0:T(8,128)(2,1)S(1)}, u32[]{:S(2)}, u32[]{:S(2)}) %all-to-all-start) | async-done | bytes 2621472 | tf_op jit(solution)/shard_map/all_to_all | solution.py:147
  59.0 1.2 copy.40
  60.3 3.6 %collective-permute-start.1 = (bf16[128,2176]{1,0:T(8,128)(2,1)S(1)}, bf16[128,2176]{1,0:T(8,128)(2,1)S(1)}, u32[]{:S(2)}, u32[]{:S(2)}) collective-permute-start(bf16[128,2176]{1,0:T(8,128)(2,1)S(1)} %fusion.1.refs_0_), channel_id=1, source_target_pairs={{2,0},{3,1},{4,2},{5,3},{6,4},{7,5},{8,6},{9,7},{10,8},{11,9},{12,... | collective-permute-start | bytes 1671176 | tf_op jit(solution)/shard_map/ppermute | solution.py:19
  63.9 1.9 %collective-permute-start = (bf16[128,2176]{1,0:T(8,128)(2,1)S(1)}, bf16[128,2176]{1,0:T(8,128)(2,1)S(1)}, u32[]{:S(2)}, u32[]{:S(2)}) collective-permute-start(bf16[128,2176]{1,0:T(8,128)(2,1)S(1)} %fusion.1.refs_0_), channel_id=1, source_target_pairs={{0,2},{1,3},{2,4},{3,5},{4,6},{5,7},{6,8},{7,9},{8,10},{9,11},{10,... | collective-permute-start | bytes 1671176 | tf_op jit(solution)/shard_map/ppermute | solution.py:19
  66.7 8.2 %collective-permute-done.1.refs_2_ = bf16[128,2176]{1,0:T(8,128)(2,1)S(1)} collective-permute-done((bf16[128,2176]{1,0:T(8,128)(2,1)S(1)}, bf16[128,2176]{1,0:T(8,128)(2,1)S(1)}, u32[]{:S(2)}, u32[]{:S(2)}) %collective-permute-start.1) | collective-permute-done | bytes 557088 | tf_op jit(solution)/shard_map/ppermute | solution.py:19
  74.9 7.6 %collective-permute-start.3 = (bf16[128,2176]{1,0:T(8,128)(2,1)S(1)}, bf16[128,2176]{1,0:T(8,128)(2,1)S(1)}, u32[]{:S(2)}, u32[]{:S(2)}) collective-permute-start(bf16[128,2176]{1,0:T(8,128)(2,1)S(1)} %collective-permute-done.1.refs_2_), channel_id=1, source_target_pairs={{2,0},{3,1},{4,2},{5,3},{6,4},{7,5},{8,6},{9,7},{10,8},{11,9},{12,... | collective-permute-start | bytes 1671176 | tf_op jit(solution)/shard_map/ppermute | solution.py:19
  82.5 1.9 %collective-permute-start.2 = (bf16[128,2176]{1,0:T(8,128)(2,1)S(1)}, bf16[128,2176]{1,0:T(8,128)(2,1)S(1)}, u32[]{:S(2)}, u32[]{:S(2)}) collective-permute-start(bf16[128,2176]{1,0:T(8,128)(2,1)S(1)} %collective-permute-done.refs_1_), channel_id=1, source_target_pairs={{0,2},{1,3},{2,4},{3,5},{4,6},{5,7},{6,8},{7,9},{8,10},{9,11},{10,... | collective-permute-start | bytes 1671176 | tf_op jit(solution)/shard_map/ppermute | solution.py:19
  86.2 5.8 %collective-permute-done.3.refs_4_ = bf16[128,2176]{1,0:T(8,128)(2,1)S(1)} collective-permute-done((bf16[128,2176]{1,0:T(8,128)(2,1)S(1)}, bf16[128,2176]{1,0:T(8,128)(2,1)S(1)}, u32[]{:S(2)}, u32[]{:S(2)}) %collective-permute-start.3) | collective-permute-done | bytes 557088 | tf_op jit(solution)/shard_map/ppermute | solution.py:19
  91.9 8.3 %collective-permute-start.5 = (bf16[128,2176]{1,0:T(8,128)(2,1)S(1)}, bf16[128,2176]{1,0:T(8,128)(2,1)S(1)}, u32[]{:S(2)}, u32[]{:S(2)}) collective-permute-start(bf16[128,2176]{1,0:T(8,128)(2,1)S(1)} %collective-permute-done.3.refs_4_), channel_id=1, source_target_pairs={{2,0},{3,1},{4,2},{5,3},{6,4},{7,5},{8,6},{9,7},{10,8},{11,9},{12,... | collective-permute-start | bytes 1671176 | tf_op jit(solution)/shard_map/ppermute | solution.py:19
  100.3 1.9 %collective-permute-start.4 = (bf16[128,2176]{1,0:T(8,128)(2,1)S(1)}, bf16[128,2176]{1,0:T(8,128)(2,1)S(1)}, u32[]{:S(2)}, u32[]{:S(2)}) collective-permute-start(bf16[128,2176]{1,0:T(8,128)(2,1)S(1)} %collective-permute-done.2.refs_3_), channel_id=1, source_target_pairs={{0,2},{1,3},{2,4},{3,5},{4,6},{5,7},{6,8},{7,9},{8,10},{9,11},{10,... | collective-permute-start | bytes 1671176 | tf_op jit(solution)/shard_map/ppermute | solution.py:19
  103.9 4.9 %collective-permute-done.5.refs_6_ = bf16[128,2176]{1,0:T(8,128)(2,1)S(1)} collective-permute-done((bf16[128,2176]{1,0:T(8,128)(2,1)S(1)}, bf16[128,2176]{1,0:T(8,128)(2,1)S(1)}, u32[]{:S(2)}, u32[]{:S(2)}) %collective-permute-start.5) | collective-permute-done | bytes 557088 | tf_op jit(solution)/shard_map/ppermute | solution.py:19
  108.8 8.1 %collective-permute-done.4.refs_5_ = bf16[128,2176]{1,0:T(8,128)(2,1)S(1)} collective-permute-done((bf16[128,2176]{1,0:T(8,128)(2,1)S(1)}, bf16[128,2176]{1,0:T(8,128)(2,1)S(1)}, u32[]{:S(2)}, u32[]{:S(2)}) %collective-permute-start.4) | collective-permute-done | bytes 557088 | tf_op jit(solution)/shard_map/ppermute | solution.py:19
  117.0 1.9 %collective-permute-start.6 = (bf16[128,2176]{1,0:T(8,128)(2,1)S(1)}, bf16[128,2176]{1,0:T(8,128)(2,1)S(1)}, u32[]{:S(2)}, u32[]{:S(2)}) collective-permute-start(bf16[128,2176]{1,0:T(8,128)(2,1)S(1)} %broadcast_select_fusion), channel_id=1, source_target_pairs={{1,3},{3,5},{5,7},{7,9},{9,11},{11,13},{13,15},{15,17},{17,19},{19... | collective-permute-start | bytes 1671176 | tf_op jit(solution)/shard_map/ppermute | solution.py:196
  120.6 10.9 %collective-permute-done.6.refs_7_ = bf16[128,2176]{1,0:T(8,128)(2,1)S(1)} collective-permute-done((bf16[128,2176]{1,0:T(8,128)(2,1)S(1)}, bf16[128,2176]{1,0:T(8,128)(2,1)S(1)}, u32[]{:S(2)}, u32[]{:S(2)}) %collective-permute-start.6) | collective-permute-done | bytes 557088 | tf_op jit(solution)/shard_map/ppermute | solution.py:196
  132.6 1.5 collective-permute-start.7
  134.3 1.4 copy.48
  135.7 3.0 %copy.45.q_ref = bf16[32,128,256]{2,1,0:T(8,128)(2,1)} copy(bf16[32,128,256]{1,2,0:T(8,128)(2,1)S(1)} %bitcast.43) | data formatting | bytes 4194304 | tf_op jit(solution)/shard_map/reshape | solution.py:182
  138.7 2.8 %collective-permute-done.7.stack_ref = bf16[8,128,2176]{2,1,0:T(8,128)(2,1)} collective-permute-done((bf16[8,128,2176]{2,1,0:T(8,128)(2,1)}, bf16[8,128,2176]{2,1,0:T(8,128)(2,1)}, u32[]{:S(2)}, u32[]{:S(2)}) %collective-permute-start.7) | collective-permute-done | bytes 4456480 | tf_op jit(solution)/shard_map/ppermute | solution.py:197
  141.5 31.9 %shard_map.86 = (bf16[128,8192]{1,0:T(8,128)(2,1)}, f32[128,128]{1,0:T(8,128)}) custom-call(s32[17]{0:T(128)} %pad_add_fusion.1.meta_ref, bf16[32,128,256]{2,1,0:T(8,128)(2,1)} %copy.45.q_ref, bf16[8,128,2176]{2,1,0:T(8,128)(2,1)} %collective-permute-done.7.stack_ref, bf16[128,2176]{1,0:T(8,128)(2,1)} %copy-done.3, bf16[128,2176]{1,0:T(8,128)(2,1)} %copy-done.5, ...), custom_call_target="tpu_custom_call" | custom-call | tf_op jit(solution)/shard_map/pallas_call | solution.py:117
  (62 shorter events, 17.1 us)
Async XLA Ops:
  0.6 173.8 %copy-start = (bf16[8192,16]{0,1:T(8,128)(2,1)S(1)}, bf16[8192,16]{0,1:T(8,128)(2,1)}, u32[]{:S(2)}) copy-start(bf16[8192,16]{0,1:T(8,128)(2,1)} %param.13) | copy-start | bytes 786436
  8.9 14.1 %copy-start.9 = (s32[32]{0:T(128)S(1)}, s32[32]{0:T(128)}, u32[]{:S(2)}) copy-start(s32[32]{0:T(128)} %param.12) | copy-start | bytes 388
  8.9 15.1 %copy-start.10 = (s32[8]{0:T(128)S(1)}, s32[8]{0:T(128)}, u32[]{:S(2)}) copy-start(s32[8]{0:T(128)} %constant.85.clone) | copy-start | bytes 100
  9.0 15.1 %copy-start.11 = (s32[8]{0:T(128)S(1)}, s32[8]{0:T(128)}, u32[]{:S(2)}) copy-start(s32[8]{0:T(128)} %constant.84.clone) | copy-start | bytes 100
  12.3 45.3 %all-to-all-start = ((bf16[128,80,128]{2,1,0:T(8,128)(2,1)}), bf16[128,80,128]{2,1,0:T(8,128)(2,1)S(1)}, u32[]{:S(2)}, u32[]{:S(2)}) async-start(bf16[128,80,128]{2,1,0:T(8,128)(2,1)} %copy.37), calls=%async_computation | async-start | bytes 5242880 | tf_op jit(solution)/shard_map/all_to_all | solution.py:147
  60.3 39.9 %copy-start.3 = (bf16[128,2176]{1,0:T(8,128)(2,1)}, bf16[128,2176]{1,0:T(8,128)(2,1)S(1)}, u32[]{:S(2)}) copy-start(bf16[128,2176]{1,0:T(8,128)(2,1)S(1)} %fusion.1.refs_0_) | copy-start | bytes 1671172
  60.3 14.6 %collective-permute-start.1 = (bf16[128,2176]{1,0:T(8,128)(2,1)S(1)}, bf16[128,2176]{1,0:T(8,128)(2,1)S(1)}, u32[]{:S(2)}, u32[]{:S(2)}) collective-permute-start(bf16[128,2176]{1,0:T(8,128)(2,1)S(1)} %fusion.1.refs_0_), channel_id=1, source_target_pairs={{2,0},{3,1},{4,2},{5,3},{6,4},{7,5},{8,6},{9,7},{10,8},{11,9},{12,... | collective-permute-start | bytes 1671176 | tf_op jit(solution)/shard_map/ppermute | solution.py:19
  63.9 18.6 %collective-permute-start = (bf16[128,2176]{1,0:T(8,128)(2,1)S(1)}, bf16[128,2176]{1,0:T(8,128)(2,1)S(1)}, u32[]{:S(2)}, u32[]{:S(2)}) collective-permute-start(bf16[128,2176]{1,0:T(8,128)(2,1)S(1)} %fusion.1.refs_0_), channel_id=1, source_target_pairs={{0,2},{1,3},{2,4},{3,5},{4,6},{5,7},{6,8},{7,9},{8,10},{9,11},{10,... | collective-permute-start | bytes 1671176 | tf_op jit(solution)/shard_map/ppermute | solution.py:19
  74.9 57.5 %copy-start.4 = (bf16[128,2176]{1,0:T(8,128)(2,1)}, bf16[128,2176]{1,0:T(8,128)(2,1)S(1)}, u32[]{:S(2)}) copy-start(bf16[128,2176]{1,0:T(8,128)(2,1)S(1)} %collective-permute-done.1.refs_2_) | copy-start | bytes 1671172
  74.9 17.0 %collective-permute-start.3 = (bf16[128,2176]{1,0:T(8,128)(2,1)S(1)}, bf16[128,2176]{1,0:T(8,128)(2,1)S(1)}, u32[]{:S(2)}, u32[]{:S(2)}) collective-permute-start(bf16[128,2176]{1,0:T(8,128)(2,1)S(1)} %collective-permute-done.1.refs_2_), channel_id=1, source_target_pairs={{2,0},{3,1},{4,2},{5,3},{6,4},{7,5},{8,6},{9,7},{10,8},{11,9},{12,... | collective-permute-start | bytes 1671176 | tf_op jit(solution)/shard_map/ppermute | solution.py:19
  82.5 49.9 %copy-start.5 = (bf16[128,2176]{1,0:T(8,128)(2,1)}, bf16[128,2176]{1,0:T(8,128)(2,1)S(1)}, u32[]{:S(2)}) copy-start(bf16[128,2176]{1,0:T(8,128)(2,1)S(1)} %collective-permute-done.refs_1_) | copy-start | bytes 1671172
  82.5 17.7 %collective-permute-start.2 = (bf16[128,2176]{1,0:T(8,128)(2,1)S(1)}, bf16[128,2176]{1,0:T(8,128)(2,1)S(1)}, u32[]{:S(2)}, u32[]{:S(2)}) collective-permute-start(bf16[128,2176]{1,0:T(8,128)(2,1)S(1)} %collective-permute-done.refs_1_), channel_id=1, source_target_pairs={{0,2},{1,3},{2,4},{3,5},{4,6},{5,7},{6,8},{7,9},{8,10},{9,11},{10,... | collective-permute-start | bytes 1671176 | tf_op jit(solution)/shard_map/ppermute | solution.py:19
  91.9 40.5 %copy-start.6 = (bf16[128,2176]{1,0:T(8,128)(2,1)}, bf16[128,2176]{1,0:T(8,128)(2,1)S(1)}, u32[]{:S(2)}) copy-start(bf16[128,2176]{1,0:T(8,128)(2,1)S(1)} %collective-permute-done.3.refs_4_) | copy-start | bytes 1671172
  91.9 16.9 %collective-permute-start.5 = (bf16[128,2176]{1,0:T(8,128)(2,1)S(1)}, bf16[128,2176]{1,0:T(8,128)(2,1)S(1)}, u32[]{:S(2)}, u32[]{:S(2)}) collective-permute-start(bf16[128,2176]{1,0:T(8,128)(2,1)S(1)} %collective-permute-done.3.refs_4_), channel_id=1, source_target_pairs={{2,0},{3,1},{4,2},{5,3},{6,4},{7,5},{8,6},{9,7},{10,8},{11,9},{12,... | collective-permute-start | bytes 1671176 | tf_op jit(solution)/shard_map/ppermute | solution.py:19
  100.3 32.2 %copy-start.7 = (bf16[128,2176]{1,0:T(8,128)(2,1)}, bf16[128,2176]{1,0:T(8,128)(2,1)S(1)}, u32[]{:S(2)}) copy-start(bf16[128,2176]{1,0:T(8,128)(2,1)S(1)} %collective-permute-done.2.refs_3_) | copy-start | bytes 1671172
  100.3 16.6 %collective-permute-start.4 = (bf16[128,2176]{1,0:T(8,128)(2,1)S(1)}, bf16[128,2176]{1,0:T(8,128)(2,1)S(1)}, u32[]{:S(2)}, u32[]{:S(2)}) collective-permute-start(bf16[128,2176]{1,0:T(8,128)(2,1)S(1)} %collective-permute-done.2.refs_3_), channel_id=1, source_target_pairs={{0,2},{1,3},{2,4},{3,5},{4,6},{5,7},{6,8},{7,9},{8,10},{9,11},{10,... | collective-permute-start | bytes 1671176 | tf_op jit(solution)/shard_map/ppermute | solution.py:19
  108.8 25.5 %copy-start.1 = (bf16[128,2176]{1,0:T(8,128)(2,1)}, bf16[128,2176]{1,0:T(8,128)(2,1)S(1)}, u32[]{:S(2)}) copy-start(bf16[128,2176]{1,0:T(8,128)(2,1)S(1)} %collective-permute-done.5.refs_6_) | copy-start | bytes 1671172
  116.9 15.5 %copy-start.2 = (bf16[128,2176]{1,0:T(8,128)(2,1)}, bf16[128,2176]{1,0:T(8,128)(2,1)S(1)}, u32[]{:S(2)}) copy-start(bf16[128,2176]{1,0:T(8,128)(2,1)S(1)} %collective-permute-done.4.refs_5_) | copy-start | bytes 1671172
  117.0 14.5 %collective-permute-start.6 = (bf16[128,2176]{1,0:T(8,128)(2,1)S(1)}, bf16[128,2176]{1,0:T(8,128)(2,1)S(1)}, u32[]{:S(2)}, u32[]{:S(2)}) collective-permute-start(bf16[128,2176]{1,0:T(8,128)(2,1)S(1)} %broadcast_select_fusion), channel_id=1, source_target_pairs={{1,3},{3,5},{5,7},{7,9},{9,11},{11,13},{13,15},{15,17},{17,19},{19... | collective-permute-start | bytes 1671176 | tf_op jit(solution)/shard_map/ppermute | solution.py:196
  131.5 1.1 copy-start.8
  132.6 9.0 %collective-permute-start.7 = (bf16[8,128,2176]{2,1,0:T(8,128)(2,1)}, bf16[8,128,2176]{2,1,0:T(8,128)(2,1)}, u32[]{:S(2)}, u32[]{:S(2)}) collective-permute-start(bf16[8,128,2176]{2,1,0:T(8,128)(2,1)} %bitcast_dynamic-update-slice_fusion), channel_id=1, source_target_pairs={{0,1},{1,0},{2,3},{3,2},{4,5},{5,4},{6,7},{7,6},{8,9},{9,8},{10,11... | collective-permute-start | bytes 13369352 | tf_op jit(solution)/shard_map/ppermute | solution.py:197
